TPU v7x, 32 devices: a whole 2x2x4 slice. The times are simulated.
32 devices in a mesh: left: 4 (over y, x), right: 8 (over z, core).
Axes of the slice: x: 2, y: 2, z: 4, core: 2. Of those that a mesh axis runs over, the one named last changes fastest.
Arguments:
- state: float32 [32, 1024, 1024], P(('left', 'right')), may hold values from -20 to 20
- left_env: bfloat16 [2, 32, 1024, 1024], P(None, ('left', 'right')), may hold values from -0.5 to 2.5
- right_env: bfloat16 [2, 32, 1024, 1024], P(None, ('left', 'right')), may hold values from -0.5 to 2.5
- site_ops: float32 [2, 4, 4], replicated, may hold values from -3 to 3
- left_live: int32 [8], replicated, may hold values from 1 to 4
- right_live: int32 [10], replicated, may hold values from 1 to 4
Outputs:
- next_vector: float32 [32, 1024, 1024], P(('left', 'right'))
- coefficients: float32 [2], replicated
All inputs are finite; a program needn't handle non-finite values.
Results may differ from a plain program's by a relative error of at most 0.0047.
Values may be sent and summed in bfloat16 or wider, within the bound.
No kernel may reach another device: no remote copies, remote signals or barrier semaphores. Data moves between devices by JAX's collectives and lax.ppermute only.
A program may use at most 64 MiB of HBM per device.

v0:
```python
import jax
import jax.numpy as jnp
from jax import lax
from jax.sharding import PartitionSpec as P

BLOCK = 256


def from_behind(block, axis, distance):
    devices = range(lax.axis_size(axis))
    route = [(i - distance, i) for i in devices if i - distance in devices]
    return lax.ppermute(block, axis, route)


def small_lookup(table, index):
    places = jnp.arange(table.shape[0], dtype=jnp.int32)
    return jnp.sum(jnp.where(places == index, table, jnp.zeros_like(table)))


def table_entry(table, row, column):
    rows = jnp.arange(table.shape[0], dtype=jnp.int32)[:, None]
    columns = jnp.arange(table.shape[1], dtype=jnp.int32)[None, :]
    return jnp.sum(jnp.where((rows == row) & (columns == column), table, jnp.zeros_like(table)))


def per_device(state, left_env, right_env, site_ops, left_live, right_live):
    pairs = site_ops.shape[1]
    sec_size = state.shape[1]
    block_size = BLOCK
    block_index = lax.axis_index("left") * lax.axis_size("right") + lax.axis_index("right")
    own_pair = block_index % pairs
    sector = block_index // pairs
    steps = (jnp.arange(pairs, dtype=jnp.int32) + 1) // 2
    own_step = small_lookup(steps, own_pair)
    positions = jnp.arange(sec_size, dtype=jnp.int32)
    row_mask = (positions < small_lookup(left_live, sector) * block_size).astype(jnp.float32)
    col_mask = (positions < small_lookup(right_live, sector + own_step) * block_size).astype(
        jnp.float32
    )
    live = row_mask[:, None] * col_mask[None, :]
    entries = float(
        state.shape[0] * sec_size * sec_size * lax.axis_size("left") * lax.axis_size("right")
    )
    masked = state[0] * live
    start_sum = lax.psum(jnp.sum(masked * masked), ("left", "right"))
    start_mean = start_sum / entries
    vector = masked / jnp.sqrt(start_mean + 1e-06)
    rounded = vector.astype(jnp.bfloat16)
    far_two = from_behind(rounded, ("left", "right"), 2)
    far_three = from_behind(rounded, ("left", "right"), 3)
    weights = []
    for offset in (2, 3):
        source_pair = (own_pair - offset) % pairs
        valid = block_index >= offset
        weights.append(
            jnp.where(
                valid, table_entry(site_ops[0], own_pair, source_pair), jnp.zeros((), jnp.float32)
            )
        )
    source = (
        weights[0] * far_two.astype(jnp.float32) + weights[1] * far_three.astype(jnp.float32)
    ).astype(jnp.bfloat16)
    part_zero = jnp.dot(source, right_env[0, 0], preferred_element_type=jnp.float32).astype(
        jnp.bfloat16
    )
    part_one = jnp.dot(rounded, right_env[1, 0], preferred_element_type=jnp.float32).astype(
        jnp.bfloat16
    )
    diag_weight = table_entry(site_ops[1], own_pair, own_pair)
    image = jnp.dot(left_env[0, 0], part_zero, preferred_element_type=jnp.float32)
    image = image + diag_weight * jnp.dot(
        left_env[1, 0], part_one, preferred_element_type=jnp.float32
    )
    image = image * live
    cross_sum, image_sum = lax.psum(
        (jnp.sum(vector * image), jnp.sum(image * image)), ("left", "right")
    )
    alpha_value = cross_sum / entries
    vector_mean = start_mean / (start_mean + 1e-06)
    residual_mean = image_sum / entries - alpha_value * alpha_value * (2.0 - vector_mean)
    residual = image - alpha_value * vector
    beta_value = jnp.sqrt(residual_mean + 1e-06)
    next_vector = residual / beta_value
    return (next_vector[None], jnp.stack([alpha_value, beta_value]))


def solution(mesh):
    in_specs = (
        P(("left", "right"), None, None),
        P(None, ("left", "right"), None, None),
        P(None, ("left", "right"), None, None),
        P(),
        P(),
        P(),
    )
    out_specs = (P(("left", "right"), None, None), P())
    return jax.shard_map(
        per_device, mesh=mesh, in_specs=in_specs, out_specs=out_specs, check_vma=False
    )
```

profile of v0, /device:TPU:14, one launch (start us, length us, event | category | flops | bytes accessed | tf_op | source)
XLA Modules:
  0.0 257.6 jit_solution(7007591481380401742)
XLA Ops:
  0.6 0.6 select_reduce_fusion
  1.9 1.3 fusion.36
  3.2 1.3 fusion.37
  5.8 5.3 %copy.8 = f32[1,1024,1024]{1,2,0:T(8,128)} copy(f32[1,1024,1024]{2,1,0:T(8,128)} %param.6) | data formatting | bytes 8388608 | tf_op args[0]
  11.2 4.1 %multiply_reduce_fusion.2 = f32[]{:T(128)} fusion(f32[1,1024,1024]{1,2,0:T(8,128)} %copy.8, f32[1024]{0:T(1024)S(1)} %get-tuple-element.13, f32[1024]{0:T(1024)S(1)} %get-tuple-element.12), kind=kLoop, calls=%fused_computation.7 | loop fusion | flops 4194303 | bytes 4202500 | tf_op jit(solution)/shard_map/reduce_sum | solution.py:45
  15.3 0.0 copy-start
  15.3 40.7 %psum.21 = f32[]{:T(128)} all-reduce(f32[]{:T(128)} %multiply_reduce_fusion.2), channel_id=1, replica_groups=mesh['left'=4,'right'=8] {'left','right'}, use_global_device_ids=true, to_apply=%region_5.6 | all-reduce | flops 1 | bytes 8 | tf_op jit(solution)/shard_map/psum | solution.py:45
  56.7 2.7 %fusion.38 = bf16[1024,1024]{0,1:T(8,128)(2,1)S(1)} fusion(f32[]{:T(128)S(6)} %sqrt.6, f32[1024]{0:T(1024)S(1)} %get-tuple-element.13, f32[1024]{0:T(1024)S(1)} %get-tuple-element.12, f32[1,1024,1024]{1,2,0:T(8,128)} %copy.8), kind=kLoop, calls=%fused_computation.50 | loop fusion | flops 4194304 | bytes 6299652 | tf_op jit(solution)/shard_map/convert_element_type | solution.py:48
  59.4 1.9 collective-permute-start.1
  61.4 3.3 %collective-permute-start = (bf16[1024,1024]{0,1:T(8,128)(2,1)S(1)}, bf16[1024,1024]{0,1:T(8,128)(2,1)}, u32[]{:S(2)}, u32[]{:S(2)}) collective-permute-start(bf16[1024,1024]{0,1:T(8,128)(2,1)S(1)} %fusion.38), channel_id=1, source_target_pairs={{0,2},{1,3},{2,4},{3,5},{4,6},{5,7},{6,8},{7,9},{8,10},{9,11},{10,... | collective-permute-start | bytes 6291464 | tf_op jit(solution)/shard_map/ppermute | solution.py:12
  64.8 0.0 copy-done
  64.8 0.8 fusion.33
  66.8 62.5 %collective-permute-done.1 = bf16[1024,1024]{0,1:T(8,128)(2,1)} collective-permute-done((bf16[1024,1024]{0,1:T(8,128)(2,1)S(1)}, bf16[1024,1024]{0,1:T(8,128)(2,1)}, u32[]{:S(2)}, u32[]{:S(2)}) %collective-permute-start.1) | collective-permute-done | bytes 2097184 | tf_op jit(solution)/shard_map/ppermute | solution.py:12
  129.2 44.9 %collective-permute-done = bf16[1024,1024]{0,1:T(8,128)(2,1)} collective-permute-done((bf16[1024,1024]{0,1:T(8,128)(2,1)S(1)}, bf16[1024,1024]{0,1:T(8,128)(2,1)}, u32[]{:S(2)}, u32[]{:S(2)}) %collective-permute-start) | collective-permute-done | bytes 2097184 | tf_op jit(solution)/shard_map/ppermute | solution.py:12
  174.2 10.0 %fusion.6 = f32[1024,1024]{1,0:T(8,128)} fusion(bf16[2,1,1024,1024]{3,2,1,0:T(8,128)(2,1)} %param.7, bf16[1024,1024]{0,1:T(8,128)(2,1)} %collective-permute-done.1, bf16[1024,1024]{0,1:T(8,128)(2,1)} %collective-permute-done, bf16[2,1,1024,1024]{3,2,1,0:T(8,128)(2,1)} %param.8, f32[]{:T(128)S(6)} %select_n.63, f32[]{:T(128)S(6)} %select_n.55), kind=kOutput, calls=%fused_computation.14 | convolution fusion | flops 4302307328 | bytes 12582920 | tf_op jit(solution)/shard_map/dot_general | solution.py:70
  184.2 13.4 %multiply_reduce_fusion.1 = (f32[]{:T(128)}, f32[]{:T(128)}, f32[1024,1024]{0,1:T(8,128)}) fusion(f32[]{:T(128)S(6)} %sqrt.6, f32[1024]{0:T(1024)S(1)} %get-tuple-element.13, f32[1024]{0:T(1024)S(1)} %get-tuple-element.12, f32[1,1024,1024]{1,2,0:T(8,128)} %copy.8, f32[1024,1024]{1,0:T(8,128)} %fusion.6, bf16[2,1,1024,1024]{3,2,1,0:T(8,128)(2,1)} %param.7, ...), kind=kOutput, calls=%fused_computation.4 | convolution fusion | flops 4310695936 | bytes 20989448 | tf_op jit(solution)/shard_map/dot_general | solution.py:71
  197.6 44.9 %all-reduce = (f32[]{:T(128)}, f32[]{:T(128)}) all-reduce(f32[]{:T(128)} %get-tuple-element.5, f32[]{:T(128)} %get-tuple-element.4), channel_id=1, replica_groups=mesh['left'=4,'right'=8] {'left','right'}, use_global_device_ids=true, to_apply=%region_11.12 | all-reduce | flops 2 | bytes 16 | tf_op jit(solution)/shard_map/psum | solution.py:75
  245.3 6.4 %divide_bitcast_fusion = f32[1,1024,1024]{1,2,0:T(8,128)} fusion(f32[1024,1024]{0,1:T(8,128)} %get-tuple-element.11, f32[]{:T(128)} %sqrt.7, f32[]{:T(128)} %div.58, f32[]{:T(128)S(6)} %sqrt.6, f32[1024]{0:T(1024)S(1)} %get-tuple-element.13, f32[1024]{0:T(1024)S(1)} %get-tuple-element.12, f32[1,1024,1024]{1,2,0:T(8,128)} %copy.8), kind=kLoop, calls=%fused_computation.2 | loop fusion | flops 6291456 | bytes 12591116 | tf_op jit(solution)/shard_map/broadcast_in_dim | solution.py:84
  251.7 5.3 %copy.9 = f32[1,1024,1024]{2,1,0:T(8,128)} copy(f32[1,1024,1024]{1,2,0:T(8,128)} %divide_bitcast_fusion) | data formatting | bytes 8388608
  257.0 0.6 pad_maximum_fusion
  (3 shorter events, 0.0 us)
Async XLA Ops:
  15.3 49.4 %copy-start = (f32[2,4,4]{2,1,0:T(4,128)S(1)}, f32[2,4,4]{2,1,0:T(4,128)}, u32[]{:S(2)}) copy-start(f32[2,4,4]{2,1,0:T(4,128)} %param.9) | copy-start | bytes 388
  59.4 69.8 %collective-permute-start.1 = (bf16[1024,1024]{0,1:T(8,128)(2,1)S(1)}, bf16[1024,1024]{0,1:T(8,128)(2,1)}, u32[]{:S(2)}, u32[]{:S(2)}) collective-permute-start(bf16[1024,1024]{0,1:T(8,128)(2,1)S(1)} %fusion.38), channel_id=1, source_target_pairs={{0,3},{1,4},{2,5},{3,6},{4,7},{5,8},{6,9},{7,10},{8,11},{9,12},{10... | collective-permute-start | bytes 6291464 | tf_op jit(solution)/shard_map/ppermute | solution.py:12
  61.4 112.8 %collective-permute-start = (bf16[1024,1024]{0,1:T(8,128)(2,1)S(1)}, bf16[1024,1024]{0,1:T(8,128)(2,1)}, u32[]{:S(2)}, u32[]{:S(2)}) collective-permute-start(bf16[1024,1024]{0,1:T(8,128)(2,1)S(1)} %fusion.38), channel_id=1, source_target_pairs={{0,2},{1,3},{2,4},{3,5},{4,6},{5,7},{6,8},{7,9},{8,10},{9,11},{10,... | collective-permute-start | bytes 6291464 | tf_op jit(solution)/shard_map/ppermute | solution.py:12
where the time goes:
time: 258 us
  waiting for transfers between devices  107 us (41%)
  blocking collectives  85.6 us (33%)
  matrix products  23.4 us (9%)
  other arithmetic  17.8 us (7%)
  local copies, waits for them, and re-layouts  10.7 us (4%)
  between operations  7.46 us (3%)
  starting transfers between devices  5.22 us (2%)
    ppermute x2, waiting for transfers between devices, from_behind(): return lax.ppermute(block, axis, route)  107 us
    psum x1, blocking collectives, per_device(): lax.psum((jnp.sum(vector * image), jnp.sum(image * image)), ('left', 'rig...  44.9 us
    psum x1, blocking collectives, per_device(): start_sum = lax.psum(jnp.sum(masked * masked), ('left', 'right'))  40.7 us
    dot_general x1, matrix products, per_device(): jnp.dot(left_env[1, 0], part_one, preferred_element_type=jnp.float32)  13.4 us
    unnamed x4, local copies, waits for them, and re-layouts  10.7 us
    dot_general x1, matrix products, per_device(): jnp.dot(left_env[0, 0], part_zero, preferred_element_type=jnp.float32)  9.99 us
    broadcast_in_dim x1, other arithmetic, per_device(): return (next_vector[None], jnp.stack([alpha_value, beta_value]))  6.39 us
    ppermute x2, starting transfers between devices, from_behind(): return lax.ppermute(block, axis, route)  5.22 us
  transfers between devices with their start and end apart: 2, of which 2 were waited for; matrix products, arithmetic and copies ran while one was open for 0% of the time, Pallas kernels for 0%

commit v1 on v0

--- a/solution.py
+++ b/solution.py
@@ -73,7 +73,7 @@
     )
     image = image * live
     cross_sum, image_sum = lax.psum(
-        (jnp.sum(vector * image), jnp.sum(image * image)), ("left", "right")
+        lax.psum((jnp.sum(vector * image), jnp.sum(image * image)), "right"), "left"
     )
     alpha_value = cross_sum / entries
     vector_mean = start_mean / (start_mean + 1e-06)

time: 258 us -> 244 us (0.946)
  the two profiles are of different devices: /device:TPU:14 before, /device:TPU:0 now
where the time goes in v1:
time: 244 us; the launch traced here: 243 us
  blocking collectives  94.5 us (39%)
  waiting for transfers between devices  81.4 us (33%)
  matrix products  23.4 us (10%)
  other arithmetic  17.8 us (7%)
  local copies, waits for them, and re-layouts  10.7 us (4%)
  starting transfers between devices  8.19 us (3%)
  between operations  7.2 us (3%)
    ppermute x2, waiting for transfers between devices, from_behind(): return lax.ppermute(block, axis, route)  81.4 us
    psum x1, blocking collectives, per_device(): start_sum = lax.psum(jnp.sum(masked * masked), ('left', 'right'))  42.2 us
    psum x1, blocking collectives, per_device(): lax.psum((jnp.sum(vector * image), jnp.sum(image * image)), 'right')  38.5 us
    psum x1, blocking collectives, per_device(): lax.psum(lax.psum((jnp.sum(vector * image), jnp.sum(image * image)), 'rig...  13.8 us
    dot_general x1, matrix products, per_device(): jnp.dot(left_env[1, 0], part_one, preferred_element_type=jnp.float32)  13.4 us
    unnamed x4, local copies, waits for them, and re-layouts  10.7 us
    dot_general x1, matrix products, per_device(): jnp.dot(left_env[0, 0], part_zero, preferred_element_type=jnp.float32)  9.99 us
    ppermute x2, starting transfers between devices, from_behind(): return lax.ppermute(block, axis, route)  8.19 us
  transfers between devices with their start and end apart: 2, of which 2 were waited for; matrix products, arithmetic and copies ran while one was open for 0% of the time, Pallas kernels for 0%

profile of v1, /device:TPU:0, one launch (start us, length us, event | category | flops | bytes accessed | tf_op | source)
XLA Modules:
  0.0 243.2 jit_solution(4456225347709528931)
XLA Ops:
  0.6 0.6 select_reduce_fusion
  1.9 1.3 fusion.36
  3.2 1.3 fusion.37
  5.8 5.3 %copy.8 = f32[1,1024,1024]{1,2,0:T(8,128)} copy(f32[1,1024,1024]{2,1,0:T(8,128)} %param.6) | data formatting | bytes 8388608 | tf_op args[0]
  11.2 4.1 %multiply_reduce_fusion.2 = f32[]{:T(128)} fusion(f32[1,1024,1024]{1,2,0:T(8,128)} %copy.8, f32[1024]{0:T(1024)S(1)} %get-tuple-element.15, f32[1024]{0:T(1024)S(1)} %get-tuple-element.14), kind=kLoop, calls=%fused_computation.7 | loop fusion | flops 4194303 | bytes 4202500 | tf_op jit(solution)/shard_map/reduce_sum | solution.py:45
  15.3 0.0 copy-start
  15.3 42.2 %psum.35 = f32[]{:T(128)} all-reduce(f32[]{:T(128)} %multiply_reduce_fusion.2), channel_id=1, replica_groups=mesh['left'=4,'right'=8] {'left','right'}, use_global_device_ids=true, to_apply=%region_5.6 | all-reduce | flops 1 | bytes 8 | tf_op jit(solution)/shard_map/psum | solution.py:45
  58.2 2.7 %fusion.38 = bf16[1024,1024]{0,1:T(8,128)(2,1)S(1)} fusion(f32[]{:T(128)S(6)} %sqrt.6, f32[1024]{0:T(1024)S(1)} %get-tuple-element.15, f32[1024]{0:T(1024)S(1)} %get-tuple-element.14, f32[1,1024,1024]{1,2,0:T(8,128)} %copy.8), kind=kLoop, calls=%fused_computation.50 | loop fusion | flops 4194304 | bytes 6299652 | tf_op jit(solution)/shard_map/convert_element_type | solution.py:48
  61.0 3.6 %collective-permute-start.1 = (bf16[1024,1024]{0,1:T(8,128)(2,1)S(1)}, bf16[1024,1024]{0,1:T(8,128)(2,1)}, u32[]{:S(2)}, u32[]{:S(2)}) collective-permute-start(bf16[1024,1024]{0,1:T(8,128)(2,1)S(1)} %fusion.38), channel_id=1, source_target_pairs={{0,3},{1,4},{2,5},{3,6},{4,7},{5,8},{6,9},{7,10},{8,11},{9,12},{10... | collective-permute-start | bytes 6291464 | tf_op jit(solution)/shard_map/ppermute | solution.py:12
  64.5 4.6 %collective-permute-start = (bf16[1024,1024]{0,1:T(8,128)(2,1)S(1)}, bf16[1024,1024]{0,1:T(8,128)(2,1)}, u32[]{:S(2)}, u32[]{:S(2)}) collective-permute-start(bf16[1024,1024]{0,1:T(8,128)(2,1)S(1)} %fusion.38), channel_id=1, source_target_pairs={{0,2},{1,3},{2,4},{3,5},{4,6},{5,7},{6,8},{7,9},{8,10},{9,11},{10,... | collective-permute-start | bytes 6291464 | tf_op jit(solution)/shard_map/ppermute | solution.py:12
  69.2 0.0 copy-done
  69.2 0.8 fusion.33
  71.2 36.4 %collective-permute-done.1 = bf16[1024,1024]{0,1:T(8,128)(2,1)} collective-permute-done((bf16[1024,1024]{0,1:T(8,128)(2,1)S(1)}, bf16[1024,1024]{0,1:T(8,128)(2,1)}, u32[]{:S(2)}, u32[]{:S(2)}) %collective-permute-start.1) | collective-permute-done | bytes 2097184 | tf_op jit(solution)/shard_map/ppermute | solution.py:12
  107.7 44.9 %collective-permute-done = bf16[1024,1024]{0,1:T(8,128)(2,1)} collective-permute-done((bf16[1024,1024]{0,1:T(8,128)(2,1)S(1)}, bf16[1024,1024]{0,1:T(8,128)(2,1)}, u32[]{:S(2)}, u32[]{:S(2)}) %collective-permute-start) | collective-permute-done | bytes 2097184 | tf_op jit(solution)/shard_map/ppermute | solution.py:12
  152.6 10.0 %fusion.6 = f32[1024,1024]{1,0:T(8,128)} fusion(bf16[2,1,1024,1024]{3,2,1,0:T(8,128)(2,1)} %param.7, bf16[1024,1024]{0,1:T(8,128)(2,1)} %collective-permute-done.1, bf16[1024,1024]{0,1:T(8,128)(2,1)} %collective-permute-done, bf16[2,1,1024,1024]{3,2,1,0:T(8,128)(2,1)} %param.8, f32[]{:T(128)S(6)} %select_n.63, f32[]{:T(128)S(6)} %select_n.55), kind=kOutput, calls=%fused_computation.14 | convolution fusion | flops 4302307328 | bytes 12582920 | tf_op jit(solution)/shard_map/dot_general | solution.py:70
  162.6 13.4 %multiply_reduce_fusion.1 = (f32[]{:T(128)}, f32[]{:T(128)}, f32[1024,1024]{0,1:T(8,128)}) fusion(f32[]{:T(128)S(6)} %sqrt.6, f32[1024]{0:T(1024)S(1)} %get-tuple-element.15, f32[1024]{0:T(1024)S(1)} %get-tuple-element.14, f32[1,1024,1024]{1,2,0:T(8,128)} %copy.8, f32[1024,1024]{1,0:T(8,128)} %fusion.6, bf16[2,1,1024,1024]{3,2,1,0:T(8,128)(2,1)} %param.7, ...), kind=kOutput, calls=%fused_computation.4 | convolution fusion | flops 4310695936 | bytes 20989448 | tf_op jit(solution)/shard_map/dot_general | solution.py:71
  176.1 38.5 %all-reduce = (f32[]{:T(128)}, f32[]{:T(128)}) all-reduce(f32[]{:T(128)} %get-tuple-element.5, f32[]{:T(128)} %get-tuple-element.4), channel_id=1, replica_groups=mesh['left'=4,'right'=8] {'right'}, use_global_device_ids=true, to_apply=%region_12.13 | all-reduce | flops 2 | bytes 16 | tf_op jit(solution)/shard_map/psum | solution.py:76
  214.5 13.8 %all-reduce.1 = (f32[]{:T(128)}, f32[]{:T(128)}) all-reduce(f32[]{:T(128)} %get-tuple-element.9, f32[]{:T(128)} %get-tuple-element.10), channel_id=1, replica_groups=mesh['left'=4,'right'=8] {'left'}, use_global_device_ids=true, to_apply=%region_13.14 | all-reduce | flops 2 | bytes 16 | tf_op jit(solution)/shard_map/psum | solution.py:75
  230.9 6.4 %divide_bitcast_fusion = f32[1,1024,1024]{1,2,0:T(8,128)} fusion(f32[1024,1024]{0,1:T(8,128)} %get-tuple-element.13, f32[]{:T(128)} %sqrt.7, f32[]{:T(128)} %div.58, f32[]{:T(128)S(6)} %sqrt.6, f32[1024]{0:T(1024)S(1)} %get-tuple-element.15, f32[1024]{0:T(1024)S(1)} %get-tuple-element.14, f32[1,1024,1024]{1,2,0:T(8,128)} %copy.8), kind=kLoop, calls=%fused_computation.2 | loop fusion | flops 6291456 | bytes 12591116 | tf_op jit(solution)/shard_map/broadcast_in_dim | solution.py:84
  237.3 5.3 %copy.9 = f32[1,1024,1024]{2,1,0:T(8,128)} copy(f32[1,1024,1024]{1,2,0:T(8,128)} %divide_bitcast_fusion) | data formatting | bytes 8388608
  242.6 0.6 pad_maximum_fusion
  (3 shorter events, 0.0 us)
Async XLA Ops:
  15.3 53.9 %copy-start = (f32[2,4,4]{2,1,0:T(4,128)S(1)}, f32[2,4,4]{2,1,0:T(4,128)}, u32[]{:S(2)}) copy-start(f32[2,4,4]{2,1,0:T(4,128)} %param.9) | copy-start | bytes 388
  61.0 46.7 %collective-permute-start.1 = (bf16[1024,1024]{0,1:T(8,128)(2,1)S(1)}, bf16[1024,1024]{0,1:T(8,128)(2,1)}, u32[]{:S(2)}, u32[]{:S(2)}) collective-permute-start(bf16[1024,1024]{0,1:T(8,128)(2,1)S(1)} %fusion.38), channel_id=1, source_target_pairs={{0,3},{1,4},{2,5},{3,6},{4,7},{5,8},{6,9},{7,10},{8,11},{9,12},{10... | collective-permute-start | bytes 6291464 | tf_op jit(solution)/shard_map/ppermute | solution.py:12
  64.5 88.1 %collective-permute-start = (bf16[1024,1024]{0,1:T(8,128)(2,1)S(1)}, bf16[1024,1024]{0,1:T(8,128)(2,1)}, u32[]{:S(2)}, u32[]{:S(2)}) collective-permute-start(bf16[1024,1024]{0,1:T(8,128)(2,1)S(1)} %fusion.38), channel_id=1, source_target_pairs={{0,2},{1,3},{2,4},{3,5},{4,6},{5,7},{6,8},{7,9},{8,10},{9,11},{10,... | collective-permute-start | bytes 6291464 | tf_op jit(solution)/shard_map/ppermute | solution.py:12
